TPU v7x, 32 devices: a whole 2x2x4 slice. The times are simulated.
32 devices in a mesh: dp: 4 (over z), ctx: 8 (over y, x, core).
Axes of the slice: x: 2, y: 2, z: 4, core: 2. Of those that a mesh axis runs over, the one named last changes fastest.
Arguments:
- tokens: bfloat16 [4, 1024, 6144], P('dp', 'ctx'), may hold values from -0.1875 to 0.1875
- cotangent: bfloat16 [4, 1024, 6144], P('dp', 'ctx'), may hold values from -6 to 6
- w_router: float32 [6144], replicated, may hold values from -2 to 2
- w_query: bfloat16 [6144, 4096], P(None, 'ctx'), may hold values from -0.078125 to 0.078125
- w_key: bfloat16 [6144, 4096], P(None, 'ctx'), may hold values from -0.078125 to 0.078125
- w_value: bfloat16 [6144, 4096], P(None, 'ctx'), may hold values from -0.078125 to 0.078125
- w_out: bfloat16 [4096, 6144], P('ctx'), may hold values from -0.09375 to 0.09375
- chosen: int32 [4, 160], P('dp', 'ctx'), may hold values from -1 to 1023, as said below
- counts: int32 [4, 8], P('dp', 'ctx'), may hold values from 12 to 20, as said below
Outputs:
- layer_out: bfloat16 [4, 1024, 6144], P('dp', 'ctx')
- grad_query: bfloat16 [6144, 4096], P('dp', 'ctx')
- grad_key: bfloat16 [6144, 4096], P('dp', 'ctx')
- grad_value: bfloat16 [6144, 4096], P('dp', 'ctx')
- grad_out: bfloat16 [4096, 6144], P('ctx', 'dp')
- grad_router: float32 [6144], replicated
Inputs may be any that keep to these rules, and one draw needn't show every extreme that they name: `chosen`: for every sequence b and device block c, the first counts[b, c] of the block's slots c * 20 to (c + 1) * 20 - 1 hold increasing positions of that device's tokens, c * 128 to (c + 1) * 128 - 1; the other slots hold -1. In every sequence the counts add up to 128, and some device's block has exactly 20 used slots.
All inputs are finite; a program needn't handle non-finite values.
Results may differ from a plain program's by a relative error of at most 0.018.
Values may be sent and summed in bfloat16 or wider, within the bound.
No kernel may reach another device: no remote copies, remote signals or barrier semaphores. Data moves between devices by JAX's collectives and lax.ppermute only.
A program may use at most 128 MiB of HBM per device.

v0:
```python
import math
import jax
import jax.numpy as jnp
from jax import lax
from jax.sharding import PartitionSpec as P

HDIM = 128
HIGHEST_PRECISION = lax.Precision.HIGHEST
ROW_CONTRACT = (((0,), (0,)), ((), ()))
COLUMN_CONTRACT = (((1,), (1,)), ((), ()))


def head_norm(values, width):
    shaped = values.reshape(values.shape[0], -1, width)
    inverse = lax.rsqrt(jnp.mean(shaped * shaped, axis=-1, keepdims=True) + 1e-06)
    return (shaped * inverse, inverse)


def norm_back(grad_hat, normal, inverse):
    return inverse * (grad_hat - normal * jnp.mean(grad_hat * normal, axis=-1, keepdims=True))


def rounded_term(part):
    return lax.optimization_barrier(part.astype(jnp.bfloat16)).astype(jnp.float32)


def body(tokens, cotangent, w_router, w_query, w_key, w_value, w_out, chosen, counts):
    length = tokens.shape[1]
    capacity = chosen.shape[1]
    inner = w_query.shape[1]
    heads_here = inner // HDIM
    scale = 1.0 / math.sqrt(HDIM)
    offset = lax.axis_index("ctx") * length
    slot_ids = lax.broadcasted_iota(jnp.int32, (capacity,), 0)
    local = chosen[0] - offset
    present = (slot_ids < counts[0, 0]) & (local >= 0) & (local < length)
    columns = lax.broadcasted_iota(jnp.int32, (capacity, length), 1)
    onehot = ((local[:, None] == columns) & present[:, None]).astype(jnp.bfloat16)
    rows = jnp.dot(onehot, tokens[0], preferred_element_type=jnp.float32)
    rows_back = jnp.dot(onehot, cotangent[0], preferred_element_type=jnp.float32)
    logits = jnp.dot(rows, w_router, precision=HIGHEST_PRECISION)
    weights = jax.nn.sigmoid(logits)
    normed = (rows * lax.rsqrt(jnp.mean(rows * rows, axis=-1, keepdims=True) + 1e-05)).astype(
        jnp.bfloat16
    )
    delta = (weights[:, None] * rows_back).astype(jnp.bfloat16)
    all_normed, all_delta, all_present = (
        lax.all_gather(normed, "ctx", axis=0, tiled=True),
        lax.all_gather(delta, "ctx", axis=0, tiled=True),
        lax.all_gather(present.astype(jnp.bfloat16), "ctx", axis=0, tiled=True),
    )
    slots = all_normed.shape[0]
    query_raw = jnp.dot(all_normed, w_query, preferred_element_type=jnp.float32)
    key_raw = jnp.dot(all_normed, w_key, preferred_element_type=jnp.float32)
    value_raw = jnp.dot(all_normed, w_value, preferred_element_type=jnp.float32)
    query_hat, query_scale = head_norm(query_raw, HDIM)
    key_hat, key_scale = head_norm(key_raw, HDIM)
    query_b = query_hat.astype(jnp.bfloat16)
    key_b = key_hat.astype(jnp.bfloat16)
    value_b = value_raw.reshape(slots, heads_here, HDIM).astype(jnp.bfloat16)
    current = lax.broadcasted_iota(jnp.int32, (slots, slots), 0)
    earlier = lax.broadcasted_iota(jnp.int32, (slots, slots), 1)
    allowed = (earlier <= current) & ((all_present[None, :] > 0.5) | (earlier == current))
    scores = jnp.einsum("ihd,jhd->hij", query_b, key_b, preferred_element_type=jnp.float32) * scale
    exponent = jnp.where(allowed[None], jnp.exp(scores), 0.0)
    attend = exponent / jnp.sum(exponent, axis=-1, keepdims=True)
    attend_b = attend.astype(jnp.bfloat16)
    mixed = jnp.einsum("hij,jhd->ihd", attend_b, value_b, preferred_element_type=jnp.float32)
    mixed = mixed.astype(jnp.bfloat16).reshape(slots, inner)
    update = lax.psum_scatter(
        rounded_term(jnp.dot(mixed, w_out, preferred_element_type=jnp.float32)).astype(
            jnp.bfloat16
        ),
        "ctx",
        scatter_dimension=0,
        tiled=True,
    ).astype(jnp.float32)
    scaled = weights[:, None] * update
    spread = jnp.dot(onehot.astype(jnp.float32).T, scaled, precision=HIGHEST_PRECISION)
    layer_out = (tokens[0].astype(jnp.float32) + spread).astype(jnp.bfloat16)[None]
    gate_back = jnp.sum(rows_back * update, axis=-1) * weights * (1.0 - weights)
    router_part = jnp.dot(gate_back, rows, precision=HIGHEST_PRECISION)
    grad_router = lax.psum(router_part, ("dp", "ctx"))
    out_term = rounded_term(
        lax.dot_general(mixed, all_delta, ROW_CONTRACT, preferred_element_type=jnp.float32)
    )
    mixed_back = lax.dot_general(
        all_delta, w_out, COLUMN_CONTRACT, preferred_element_type=jnp.float32
    )
    mixed_back = mixed_back.astype(jnp.bfloat16).reshape(slots, heads_here, HDIM)
    attend_back = jnp.einsum(
        "ihd,jhd->hij", mixed_back, value_b, preferred_element_type=jnp.float32
    )
    inner_sum = jnp.sum(attend * attend_back, axis=-1, keepdims=True)
    scores_back = (attend * (attend_back - inner_sum) * scale).astype(jnp.bfloat16)
    value_back = jnp.einsum(
        "hij,ihd->jhd", attend_b, mixed_back, preferred_element_type=jnp.float32
    )
    value_back = value_back.astype(jnp.bfloat16).reshape(slots, inner)
    qhat_back = jnp.einsum("hij,jhd->ihd", scores_back, key_b, preferred_element_type=jnp.float32)
    khat_back = jnp.einsum("hij,ihd->jhd", scores_back, query_b, preferred_element_type=jnp.float32)
    query_back = (
        norm_back(qhat_back, query_hat, query_scale).astype(jnp.bfloat16).reshape(slots, inner)
    )
    key_back = norm_back(khat_back, key_hat, key_scale).astype(jnp.bfloat16).reshape(slots, inner)
    query_term = rounded_term(
        lax.dot_general(all_normed, query_back, ROW_CONTRACT, preferred_element_type=jnp.float32)
    )
    key_term = rounded_term(
        lax.dot_general(all_normed, key_back, ROW_CONTRACT, preferred_element_type=jnp.float32)
    )
    value_term = rounded_term(
        lax.dot_general(all_normed, value_back, ROW_CONTRACT, preferred_element_type=jnp.float32)
    )
    grad_query, grad_key, grad_value, grad_out = (
        lax.psum_scatter(
            query_term.astype(jnp.bfloat16), "dp", scatter_dimension=0, tiled=True
        ).astype(jnp.float32),
        lax.psum_scatter(
            key_term.astype(jnp.bfloat16), "dp", scatter_dimension=0, tiled=True
        ).astype(jnp.float32),
        lax.psum_scatter(
            value_term.astype(jnp.bfloat16), "dp", scatter_dimension=0, tiled=True
        ).astype(jnp.float32),
        lax.psum_scatter(
            out_term.astype(jnp.bfloat16), "dp", scatter_dimension=1, tiled=True
        ).astype(jnp.float32),
    )
    return (
        layer_out,
        grad_query.astype(jnp.bfloat16),
        grad_key.astype(jnp.bfloat16),
        grad_value.astype(jnp.bfloat16),
        grad_out.astype(jnp.bfloat16),
        grad_router,
    )


def solution(mesh):
    in_specs = (
        P("dp", "ctx", None),
        P("dp", "ctx", None),
        P(),
        P(None, "ctx"),
        P(None, "ctx"),
        P(None, "ctx"),
        P("ctx", None),
        P("dp", "ctx"),
        P("dp", "ctx"),
    )
    out_specs = (
        P("dp", "ctx", None),
        P("dp", "ctx"),
        P("dp", "ctx"),
        P("dp", "ctx"),
        P("ctx", "dp"),
        P(),
    )
    return jax.shard_map(body, mesh=mesh, in_specs=in_specs, out_specs=out_specs, check_vma=False)
```

profile of v0, /device:TPU:0, one launch (start us, length us, event | category | flops | bytes accessed | tf_op | source)
XLA Modules:
  0.0 630.2 jit_solution(3186163892697100419)
XLA Ops:
  8.0 0.7 fusion.88
  8.7 1.9 multiply_reduce_fusion.1
  10.6 0.9 fusion.31
  11.6 0.7 fusion.89
  13.1 15.3 %all-reduce = bf16[160]{0:T(256)(128)(2,1)S(1)} all-reduce(bf16[160]{0:T(256)(128)(2,1)S(1)} %dynamic-update-slice), channel_id=1, replica_groups=mesh['dp'=4,'ctx'=8] {'ctx'}, use_global_device_ids=true, to_apply=%add | all-reduce | flops 160 | bytes 640
  28.4 0.7 fusion.54
  29.2 14.3 %all-gather.5.cloned.1.call-done = bf16[8,20,6144]{2,1,0:T(8,128)(2,1)} async-done(((bf16[1,20,6144]{2,1,0:T(8,128)(2,1)}), bf16[8,20,6144]{2,1,0:T(8,128)(2,1)}) %all-gather.5.cloned.1.call-update) | async-done | bytes 1966096 | tf_op jit(solution)/shard_map/all_gather | solution.py:48
  43.4 2.6 reshape.127
  46.0 4.8 fusion.16
  50.8 4.8 fusion.103
  55.7 1.9 fusion.102
  57.6 1.8 reshape.116
  59.4 1.9 multiply_reduce_fusion.5
  61.3 1.0 copy.67
  62.2 1.8 reshape.117
  64.0 1.9 multiply_reduce_fusion.4
  65.9 1.0 copy.69
  66.9 2.4 fusion.28
  69.2 1.5 fusion.14
  70.8 0.6 copy-done.7
  71.4 5.4 convolution_convert_fusion.4
  76.8 30.2 %fusion = bf16[24,6144]{1,0:T(8,128)(2,1)} fusion(bf16[160,6144]{1,0:T(8,128)(2,1)} %convolution_convert_fusion.4), kind=kCustom, calls=%all-reduce-scatter | all-reduce-scatter fusion | flops 1179649 | bytes 2261504
  106.9 2.0 collective-permute-start
  108.9 1.5 slice
  110.5 3.2 collective-permute-start.1
  113.7 2.3 fusion.21
  116.6 9.6 %concatenate = bf16[52,6144]{1,0:T(8,128)(2,1)} concatenate(bf16[4,6144]{1,0:T(4,128)(2,1)} %collective-permute-done.1, bf16[24,6144]{1,0:T(8,128)(2,1)} %collective-permute-done, bf16[24,6144]{1,0:T(8,128)(2,1)} %fusion), dimensions={0} | concatenate | bytes 1277952
  126.2 2.8 fusion.26
  129.1 30.2 %all-gather.7.cloned.1.call-done = bf16[8,20,6144]{2,1,0:T(8,128)(2,1)} async-done(((bf16[1,20,6144]{2,1,0:T(8,128)(2,1)}), bf16[8,20,6144]{2,1,0:T(8,128)(2,1)}) %all-gather.7.cloned.1.call-update) | async-done | bytes 1966096 | tf_op jit(solution)/shard_map/all_gather | solution.py:49
  159.3 4.0 reshape.129
  163.3 6.0 convolution_convert_fusion
  169.6 5.8 fusion.17
  175.4 0.7 copy-done.10
  176.1 1.1 fusion.48
  177.2 2.6 multiply_reduce_fusion.3
  179.8 5.7 convolution_convert_fusion.3
  185.6 2.4 multiply_reduce_fusion.2
  188.0 5.6 convolution_convert_fusion.2
  193.6 0.8 copy-done.11
  194.7 4.4 convolution_convert_fusion.1
  199.2 1.0 copy-done.3
  200.2 0.4 fusion.77
  200.6 47.0 %psum.7 = f32[6144]{0:T(1024)} all-reduce(f32[6144]{0:T(1024)S(1)} %bitcast.169), channel_id=1, replica_groups=mesh['dp'=4,'ctx'=8] {'dp','ctx'}, use_global_device_ids=true, to_apply=%region_13.14 | all-reduce | flops 6144 | bytes 49152 | tf_op jit(solution)/shard_map/psum | solution.py:83
  247.6 4.4 fusion.3
  252.0 29.3 %reduce-scatter.13.cloned.1.call-done = bf16[512,1536]{1,0:T(8,128)(2,1)} async-done(((bf16[512,6144]{1,0:T(8,128)(2,1)}), bf16[512,1536]{1,0:T(8,128)(2,1)}) %reduce-scatter.13.cloned.1.call-update) | async-done | bytes 1572880 | tf_op jit(solution)/shard_map/reduce_scatter | solution.py:125
  281.3 114.0 %reduce-scatter.7.cloned.1.call-done = bf16[1536,512]{1,0:T(8,128)(2,1)} async-done(((bf16[6144,512]{1,0:T(8,128)(2,1)}), bf16[1536,512]{1,0:T(8,128)(2,1)}) %reduce-scatter.7.cloned.1.call-update) | async-done | bytes 1572880 | tf_op jit(solution)/shard_map/reduce_scatter | solution.py:116
  395.3 114.0 %reduce-scatter.9.cloned.1.call-done = bf16[1536,512]{1,0:T(8,128)(2,1)} async-done(((bf16[6144,512]{1,0:T(8,128)(2,1)}), bf16[1536,512]{1,0:T(8,128)(2,1)}) %reduce-scatter.9.cloned.1.call-update) | async-done | bytes 1572880 | tf_op jit(solution)/shard_map/reduce_scatter | solution.py:119
  509.3 114.0 %reduce-scatter.11.cloned.1.call-done = bf16[1536,512]{1,0:T(8,128)(2,1)} async-done(((bf16[6144,512]{1,0:T(8,128)(2,1)}), bf16[1536,512]{1,0:T(8,128)(2,1)}) %reduce-scatter.11.cloned.1.call-update) | async-done | bytes 1572880 | tf_op jit(solution)/shard_map/reduce_scatter | solution.py:122
  (61 shorter events, 1.1 us)
Async XLA Ops:
  7.2 119.0 %copy-start = (bf16[1,128,6144]{2,1,0:T(8,128)(2,1)S(1)}, bf16[1,128,6144]{2,1,0:T(8,128)(2,1)}, u32[]{:S(2)}) copy-start(bf16[1,128,6144]{2,1,0:T(8,128)(2,1)} %param.10) | copy-start | bytes 4718596
  7.2 4.4 copy-start.18
  7.2 36.2 %all-gather.5.cloned.1.call-start = ((), (), s32[]{:S(2)}) async-start(), calls=%async_computation.8 | async-start | bytes 2654208 | tf_op jit(solution)/shard_map/all_gather | solution.py:48
  8.7 20.5 %copy-start.12 = (pred[20]{0:T(512)(128)(4,1)}, pred[20]{0:T(512)(128)(4,1)S(1)}, u32[]{:S(2)}) copy-start(pred[20]{0:T(512)(128)(4,1)S(1)} %get-tuple-element.7) | copy-start | bytes 64
  8.7 20.5 %copy-start.14 = (s32[20]{0:T(128)}, s32[20]{0:T(128)S(1)}, u32[]{:S(2)}) copy-start(s32[20]{0:T(128)S(1)} %get-tuple-element.8) | copy-start | bytes 244
  10.6 18.6 %copy-start.2 = (f32[20,6144]{1,0:T(8,128)}, f32[20,6144]{1,0:T(8,128)S(1)}, u32[]{:S(2)}) copy-start(f32[20,6144]{1,0:T(8,128)S(1)} %get-tuple-element.14) | copy-start | bytes 1474564
  11.5 147.8 %all-gather.7.cloned.1.call-start = ((), (), s32[]{:S(2)}) async-start(), calls=%async_computation.9 | async-start | bytes 2654208 | tf_op jit(solution)/shard_map/all_gather | solution.py:49
  46.0 9.6 %slice-start = ((s8[6291456]{0:T(1024)(128)(4,1)}), s8[4194304]{0:T(1024)(128)(4,1)S(1)}, s32[]{:S(2)}) async-start(s8[6291456]{0:T(1024)(128)(4,1)} %bitcast.167), calls=%async_computation.10 | async-start | bytes 8388608
  50.8 4.8 slice-start.1
  70.7 0.7 copy-start.7
  76.8 49.5 %copy-start.13 = (pred[20]{0:T(512)(128)(4,1)S(1)}, pred[20]{0:T(512)(128)(4,1)}, u32[]{:S(2)}) copy-start(pred[20]{0:T(512)(128)(4,1)} %copy-done.12) | copy-start | bytes 64
  76.8 49.5 %copy-start.15 = (s32[20]{0:T(128)S(1)}, s32[20]{0:T(128)}, u32[]{:S(2)}) copy-start(s32[20]{0:T(128)} %copy-done.14) | copy-start | bytes 244
  106.9 9.7 %collective-permute-start = (bf16[24,6144]{1,0:T(8,128)(2,1)}, bf16[24,6144]{1,0:T(8,128)(2,1)}, u32[]{:S(2)}, u32[]{:S(2)}) collective-permute-start(bf16[24,6144]{1,0:T(8,128)(2,1)} %fusion), channel_id=1, source_target_pairs={{0,1},{1,2},{2,3},{3,4},{4,5},{5,6},{6,7},{8,9},{9,10},{10,11},{11... | collective-permute-start | bytes 884744
  110.5 6.2 collective-permute-start.1
  129.0 34.3 %copy-start.8 = (bf16[4,20,8,128]{3,2,1,0:T(8,128)(2,1)S(1)}, bf16[4,20,8,128]{3,2,1,0:T(8,128)(2,1)}, u32[]{:S(2)}) copy-start(bf16[4,20,8,128]{3,2,1,0:T(8,128)(2,1)} %copy-done.7) | copy-start | bytes 491524
  129.1 152.3 %reduce-scatter.13.cloned.1.call-start = ((), (), s32[]{:S(2)}) async-start(), calls=%async_computation.7 | async-start | bytes 7864320 | tf_op jit(solution)/shard_map/reduce_scatter | solution.py:125
  169.4 6.8 %copy-start.9 = (bf16[20,4,8,128]{3,2,1,0:T(8,128)(2,1)S(1)}, bf16[20,4,8,128]{3,2,1,0:T(8,128)(2,1)}, u32[]{:S(2)}) copy-start(bf16[20,4,8,128]{3,2,1,0:T(8,128)(2,1)} %fusion.16) | copy-start | bytes 491524
  169.4 7.8 %copy-start.4 = (f32[160,512]{1,0:T(8,128)S(1)}, f32[160,512]{1,0:T(8,128)}, u32[]{:S(2)}) copy-start(f32[160,512]{1,0:T(8,128)} %fusion.103) | copy-start | bytes 983044
  169.4 7.8 %copy-start.5 = (f32[160,512]{1,0:T(8,128)S(1)}, f32[160,512]{1,0:T(8,128)}, u32[]{:S(2)}) copy-start(f32[160,512]{1,0:T(8,128)} %fusion.102) | copy-start | bytes 983044
  169.4 7.8 %copy-start.6 = (f32[4,160,160]{1,2,0:T(8,128)S(1)}, f32[4,160,160]{1,2,0:T(8,128)}, u32[]{:S(2)}) copy-start(f32[4,160,160]{1,2,0:T(8,128)} %fusion.28) | copy-start | bytes 1228804
  169.4 225.9 %reduce-scatter.7.cloned.1.call-start = ((), (), s32[]{:S(2)}) async-start(), calls=%async_computation.4 | async-start | bytes 7864320 | tf_op jit(solution)/shard_map/reduce_scatter | solution.py:116
  175.4 0.7 copy-start.10
  185.5 323.8 %reduce-scatter.9.cloned.1.call-start = ((), (), s32[]{:S(2)}) async-start(), calls=%async_computation.5 | async-start | bytes 7864320 | tf_op jit(solution)/shard_map/reduce_scatter | solution.py:119
  193.5 0.9 copy-start.11
  193.6 429.8 %reduce-scatter.11.cloned.1.call-start = ((), (), s32[]{:S(2)}) async-start(), calls=%async_computation.6 | async-start | bytes 7864320 | tf_op jit(solution)/shard_map/reduce_scatter | solution.py:122
  199.1 1.1 copy-start.3
  199.1 1.1 copy-start.16
  199.1 1.1 copy-start.17
  199.2 424.2 %copy-start.1 = (bf16[1,128,6144]{2,1,0:T(8,128)(2,1)S(1)}, bf16[1,128,6144]{2,1,0:T(8,128)(2,1)}, u32[]{:S(2)}) copy-start(bf16[1,128,6144]{2,1,0:T(8,128)(2,1)} %param.10) | copy-start | bytes 4718596
Sparse Core Ops, SparseCore 0:
  11.6 31.7 all-gather.4
  129.2 30.0 all-gather.6
  169.5 111.7 reduce-scatter.12
  284.1 111.2 reduce-scatter.6
  398.0 111.2 reduce-scatter.8
  512.1 111.2 reduce-scatter.10
where the time goes:
time: 632 us; the launch traced here: 630 us
  waiting for transfers between devices  416 us (66%)
  blocking collectives  92.5 us (15%)
  matrix products  66.3 us (10%)
  local copies, waits for them, and re-layouts  27.4 us (4%)
  between operations  16.4 us (3%)
    reduce_scatter x1, waiting for transfers between devices, body(): lax.psum_scatter(value_term.astype(jnp.bfloat16), 'dp', scatter_dimension...  114 us
    reduce_scatter x1, waiting for transfers between devices, body(): lax.psum_scatter(key_term.astype(jnp.bfloat16), 'dp', scatter_dimension=0...  114 us
    reduce_scatter x1, waiting for transfers between devices, body(): lax.psum_scatter(query_term.astype(jnp.bfloat16), 'dp', scatter_dimension...  114 us
    psum x1, blocking collectives, body(): grad_router = lax.psum(router_part, ('dp', 'ctx'))  47 us
    unnamed x2, blocking collectives  45.5 us
    all_gather x1, waiting for transfers between devices, body(): lax.all_gather(delta, 'ctx', axis=0, tiled=True)  30.2 us
    reduce_scatter x1, waiting for transfers between devices, body(): lax.psum_scatter(out_term.astype(jnp.bfloat16), 'dp', scatter_dimension=1...  29.3 us
    unnamed x49, local copies, waits for them, and re-layouts  21.9 us
  transfers between devices with their start and end apart: 8, of which 6 were waited for; matrix products, arithmetic and copies ran while one was open for 6% of the time, Pallas kernels for 0%

commit v1 on v0

--- a/solution.py
+++ b/solution.py
@@ -80,7 +80,7 @@
     layer_out = (tokens[0].astype(jnp.float32) + spread).astype(jnp.bfloat16)[None]
     gate_back = jnp.sum(rows_back * update, axis=-1) * weights * (1.0 - weights)
     router_part = jnp.dot(gate_back, rows, precision=HIGHEST_PRECISION)
-    grad_router = lax.psum(router_part, ("dp", "ctx"))
+    grad_router = jnp.sum(lax.all_gather(router_part, ("dp", "ctx")), axis=0)
     out_term = rounded_term(
         lax.dot_general(mixed, all_delta, ROW_CONTRACT, preferred_element_type=jnp.float32)
     )

time: 632 us -> 635 us (level)
    all_gather x0 -> x1, blocking collectives: none -> 51.3 us  [body(): grad_router = jnp.sum(lax.all_gather(router_part, ('dp', 'ctx')), axis=0)]
    psum x1 -> x0, blocking collectives: 47 us -> none  [body(): grad_router = lax.psum(router_part, ('dp', 'ctx'))]
    unnamed x49 -> x51, local copies, waits for them, and re-layouts: 21.9 us -> 21.7 us
  transfers between devices with their start and end apart: 8 -> 8, of which waited for: 6 -> 6; matrix products, arithmetic and copies ran while one was open for 6% -> 7% of each run, Pallas kernels for 0% -> 0%
where the time goes in v1:
time: 635 us; the launch traced here: 633 us
  waiting for transfers between devices  412 us (65%)
  blocking collectives  96.8 us (15%)
  matrix products  65.7 us (10%)
  local copies, waits for them, and re-layouts  29.5 us (5%)
  between operations  16.4 us (3%)
  other arithmetic  7.84 us (1%)
    reduce_scatter x1, waiting for transfers between devices, body(): lax.psum_scatter(query_term.astype(jnp.bfloat16), 'dp', scatter_dimension...  114 us
    reduce_scatter x1, waiting for transfers between devices, body(): lax.psum_scatter(value_term.astype(jnp.bfloat16), 'dp', scatter_dimension...  114 us
    reduce_scatter x1, waiting for transfers between devices, body(): lax.psum_scatter(key_term.astype(jnp.bfloat16), 'dp', scatter_dimension=0...  114 us
    all_gather x1, blocking collectives, body(): grad_router = jnp.sum(lax.all_gather(router_part, ('dp', 'ctx')), axis=0)  51.3 us
    unnamed x2, blocking collectives  45.5 us
    all_gather x1, waiting for transfers between devices, body(): lax.all_gather(delta, 'ctx', axis=0, tiled=True)  30.3 us
    reduce_scatter x1, waiting for transfers between devices, body(): lax.psum_scatter(out_term.astype(jnp.bfloat16), 'dp', scatter_dimension=1...  24.2 us
    unnamed x51, local copies, waits for them, and re-layouts  21.7 us
  transfers between devices with their start and end apart: 8, of which 6 were waited for; matrix products, arithmetic and copies ran while one was open for 7% of the time, Pallas kernels for 0%

profile of v1, /device:TPU:0, one launch (start us, length us, event | category | flops | bytes accessed | tf_op | source)
XLA Modules:
  0.0 633.3 jit_solution(12831897544611512511)
XLA Ops:
  8.0 0.7 fusion.88
  8.7 1.9 multiply_reduce_fusion.1
  10.6 0.9 fusion.31
  13.1 15.3 %all-reduce = bf16[160]{0:T(256)(128)(2,1)S(1)} all-reduce(bf16[160]{0:T(256)(128)(2,1)S(1)} %dynamic-update-slice), channel_id=1, replica_groups=mesh['dp'=4,'ctx'=8] {'ctx'}, use_global_device_ids=true, to_apply=%add | all-reduce | flops 160 | bytes 640
  28.4 0.7 fusion.54
  29.1 14.4 %all-gather.6.cloned.1.call-done = bf16[8,20,6144]{2,1,0:T(8,128)(2,1)} async-done(((bf16[1,20,6144]{2,1,0:T(8,128)(2,1)}), bf16[8,20,6144]{2,1,0:T(8,128)(2,1)}) %all-gather.6.cloned.1.call-update) | async-done | bytes 1966096 | tf_op jit(solution)/shard_map/all_gather | solution.py:48
  43.5 2.6 reshape.128
  46.1 4.8 fusion.16
  50.9 4.8 fusion.103
  55.7 1.9 fusion.102
  57.7 1.8 reshape.116
  59.5 1.9 multiply_reduce_fusion.5
  61.3 1.0 copy.83
  62.3 1.8 reshape.117
  64.1 1.9 multiply_reduce_fusion.4
  66.0 1.0 copy.85
  67.0 2.4 fusion.28
  69.3 1.5 fusion.14
  70.8 0.7 copy-done.8
  71.5 5.3 convolution_convert_fusion.4
  76.8 30.2 %fusion = bf16[24,6144]{1,0:T(8,128)(2,1)} fusion(bf16[160,6144]{1,0:T(8,128)(2,1)} %convolution_convert_fusion.4), kind=kCustom, calls=%all-reduce-scatter | all-reduce-scatter fusion | flops 1179649 | bytes 2261504
  107.0 2.0 collective-permute-start
  109.0 1.5 slice
  110.5 3.2 collective-permute-start.1
  113.7 2.3 fusion.21
  116.6 9.5 %concatenate = bf16[52,6144]{1,0:T(8,128)(2,1)} concatenate(bf16[4,6144]{1,0:T(4,128)(2,1)} %collective-permute-done.1, bf16[24,6144]{1,0:T(8,128)(2,1)} %collective-permute-done, bf16[24,6144]{1,0:T(8,128)(2,1)} %fusion), dimensions={0} | concatenate | bytes 1277952
  126.1 2.8 fusion.26
  129.0 30.3 %all-gather.8.cloned.1.call-done = bf16[8,20,6144]{2,1,0:T(8,128)(2,1)} async-done(((bf16[1,20,6144]{2,1,0:T(8,128)(2,1)}), bf16[8,20,6144]{2,1,0:T(8,128)(2,1)}) %all-gather.8.cloned.1.call-update) | async-done | bytes 1966096 | tf_op jit(solution)/shard_map/all_gather | solution.py:49
  159.3 4.0 reshape.130
  163.3 6.0 convolution_convert_fusion
  169.6 5.8 fusion.17
  175.4 0.7 copy-done.11
  176.1 1.1 fusion.48
  177.2 2.6 multiply_reduce_fusion.3
  179.8 5.6 convolution_convert_fusion.3
  185.5 2.4 multiply_reduce_fusion.2
  187.9 5.6 convolution_convert_fusion.2
  193.5 0.8 copy-done.12
  194.6 4.4 convolution_convert_fusion.1
  199.1 1.0 copy-done.3
  200.5 51.3 %all-gather = f32[196608]{0:T(1024)} all-gather(f32[6144]{0:T(1024)S(1)} %bitcast.169), channel_id=2, replica_groups=mesh['dp'=4,'ctx'=8] {'dp','ctx'}, dimensions={0}, use_global_device_ids=true | all-gather | bytes 811008 | tf_op jit(solution)/shard_map/all_gather | solution.py:83
  251.8 2.3 reshape.123
  254.1 1.8 reduce_sum.89
  255.9 3.8 fusion.3
  259.7 24.2 %reduce-scatter.13.cloned.1.call-done = bf16[512,1536]{1,0:T(8,128)(2,1)} async-done(((bf16[512,6144]{1,0:T(8,128)(2,1)}), bf16[512,1536]{1,0:T(8,128)(2,1)}) %reduce-scatter.13.cloned.1.call-update) | async-done | bytes 1572880 | tf_op jit(solution)/shard_map/reduce_scatter | solution.py:125
  283.9 114.5 %reduce-scatter.7.cloned.1.call-done = bf16[1536,512]{1,0:T(8,128)(2,1)} async-done(((bf16[6144,512]{1,0:T(8,128)(2,1)}), bf16[1536,512]{1,0:T(8,128)(2,1)}) %reduce-scatter.7.cloned.1.call-update) | async-done | bytes 1572880 | tf_op jit(solution)/shard_map/reduce_scatter | solution.py:116
  398.4 114.0 %reduce-scatter.9.cloned.1.call-done = bf16[1536,512]{1,0:T(8,128)(2,1)} async-done(((bf16[6144,512]{1,0:T(8,128)(2,1)}), bf16[1536,512]{1,0:T(8,128)(2,1)}) %reduce-scatter.9.cloned.1.call-update) | async-done | bytes 1572880 | tf_op jit(solution)/shard_map/reduce_scatter | solution.py:119
  512.4 114.0 %reduce-scatter.11.cloned.1.call-done = bf16[1536,512]{1,0:T(8,128)(2,1)} async-done(((bf16[6144,512]{1,0:T(8,128)(2,1)}), bf16[1536,512]{1,0:T(8,128)(2,1)}) %reduce-scatter.11.cloned.1.call-update) | async-done | bytes 1572880 | tf_op jit(solution)/shard_map/reduce_scatter | solution.py:122
  (65 shorter events, 2.1 us)
Async XLA Ops:
  7.2 119.0 %copy-start = (bf16[1,128,6144]{2,1,0:T(8,128)(2,1)S(1)}, bf16[1,128,6144]{2,1,0:T(8,128)(2,1)}, u32[]{:S(2)}) copy-start(bf16[1,128,6144]{2,1,0:T(8,128)(2,1)} %param.10) | copy-start | bytes 4718596
  7.2 4.4 copy-start.19
  7.2 36.3 %all-gather.6.cloned.1.call-start = ((), (), s32[]{:S(2)}) async-start(), calls=%async_computation.8 | async-start | bytes 2654208 | tf_op jit(solution)/shard_map/all_gather | solution.py:48
  8.7 20.4 %copy-start.13 = (pred[20]{0:T(512)(128)(4,1)}, pred[20]{0:T(512)(128)(4,1)S(1)}, u32[]{:S(2)}) copy-start(pred[20]{0:T(512)(128)(4,1)S(1)} %get-tuple-element.7) | copy-start | bytes 64
  8.7 20.4 %copy-start.15 = (s32[20]{0:T(128)}, s32[20]{0:T(128)S(1)}, u32[]{:S(2)}) copy-start(s32[20]{0:T(128)S(1)} %get-tuple-element.8) | copy-start | bytes 244
  10.6 18.5 %copy-start.2 = (f32[20,6144]{1,0:T(8,128)}, f32[20,6144]{1,0:T(8,128)S(1)}, u32[]{:S(2)}) copy-start(f32[20,6144]{1,0:T(8,128)S(1)} %get-tuple-element.14) | copy-start | bytes 1474564
  11.5 147.8 %all-gather.8.cloned.1.call-start = ((), (), s32[]{:S(2)}) async-start(), calls=%async_computation.9 | async-start | bytes 2654208 | tf_op jit(solution)/shard_map/all_gather | solution.py:49
  46.1 9.7 %slice-start = ((s8[6291456]{0:T(1024)(128)(4,1)}), s8[4194304]{0:T(1024)(128)(4,1)S(1)}, s32[]{:S(2)}) async-start(s8[6291456]{0:T(1024)(128)(4,1)} %bitcast.167), calls=%async_computation.10 | async-start | bytes 8388608
  50.9 4.8 slice-start.1
  70.8 0.7 copy-start.8
  76.8 49.3 %copy-start.14 = (pred[20]{0:T(512)(128)(4,1)S(1)}, pred[20]{0:T(512)(128)(4,1)}, u32[]{:S(2)}) copy-start(pred[20]{0:T(512)(128)(4,1)} %copy-done.13) | copy-start | bytes 64
  76.8 49.3 %copy-start.16 = (s32[20]{0:T(128)S(1)}, s32[20]{0:T(128)}, u32[]{:S(2)}) copy-start(s32[20]{0:T(128)} %copy-done.15) | copy-start | bytes 244
  107.0 9.6 %collective-permute-start = (bf16[24,6144]{1,0:T(8,128)(2,1)}, bf16[24,6144]{1,0:T(8,128)(2,1)}, u32[]{:S(2)}, u32[]{:S(2)}) collective-permute-start(bf16[24,6144]{1,0:T(8,128)(2,1)} %fusion), channel_id=1, source_target_pairs={{0,1},{1,2},{2,3},{3,4},{4,5},{5,6},{6,7},{8,9},{9,10},{10,11},{11... | collective-permute-start | bytes 884744
  110.5 6.1 collective-permute-start.1
  128.9 34.3 %copy-start.9 = (bf16[4,20,8,128]{3,2,1,0:T(8,128)(2,1)S(1)}, bf16[4,20,8,128]{3,2,1,0:T(8,128)(2,1)}, u32[]{:S(2)}) copy-start(bf16[4,20,8,128]{3,2,1,0:T(8,128)(2,1)} %copy-done.8) | copy-start | bytes 491524
  129.0 155.0 %reduce-scatter.13.cloned.1.call-start = ((), (), s32[]{:S(2)}) async-start(), calls=%async_computation.7 | async-start | bytes 7864320 | tf_op jit(solution)/shard_map/reduce_scatter | solution.py:125
  169.3 6.7 %copy-start.10 = (bf16[20,4,8,128]{3,2,1,0:T(8,128)(2,1)S(1)}, bf16[20,4,8,128]{3,2,1,0:T(8,128)(2,1)}, u32[]{:S(2)}) copy-start(bf16[20,4,8,128]{3,2,1,0:T(8,128)(2,1)} %fusion.16) | copy-start | bytes 491524
  169.3 7.8 %copy-start.5 = (f32[160,512]{1,0:T(8,128)S(1)}, f32[160,512]{1,0:T(8,128)}, u32[]{:S(2)}) copy-start(f32[160,512]{1,0:T(8,128)} %fusion.103) | copy-start | bytes 983044
  169.3 7.8 %copy-start.6 = (f32[160,512]{1,0:T(8,128)S(1)}, f32[160,512]{1,0:T(8,128)}, u32[]{:S(2)}) copy-start(f32[160,512]{1,0:T(8,128)} %fusion.102) | copy-start | bytes 983044
  169.4 7.8 %copy-start.7 = (f32[4,160,160]{1,2,0:T(8,128)S(1)}, f32[4,160,160]{1,2,0:T(8,128)}, u32[]{:S(2)}) copy-start(f32[4,160,160]{1,2,0:T(8,128)} %fusion.28) | copy-start | bytes 1228804
  169.4 229.0 %reduce-scatter.7.cloned.1.call-start = ((), (), s32[]{:S(2)}) async-start(), calls=%async_computation.4 | async-start | bytes 7864320 | tf_op jit(solution)/shard_map/reduce_scatter | solution.py:116
  175.4 0.7 copy-start.11
  185.4 327.0 %reduce-scatter.9.cloned.1.call-start = ((), (), s32[]{:S(2)}) async-start(), calls=%async_computation.5 | async-start | bytes 7864320 | tf_op jit(solution)/shard_map/reduce_scatter | solution.py:119
  193.5 0.9 copy-start.12
  193.5 432.9 %reduce-scatter.11.cloned.1.call-start = ((), (), s32[]{:S(2)}) async-start(), calls=%async_computation.6 | async-start | bytes 7864320 | tf_op jit(solution)/shard_map/reduce_scatter | solution.py:122
  199.1 1.1 copy-start.3
  199.1 1.1 copy-start.17
  199.1 1.1 copy-start.18
  199.1 56.8 %copy-start.4 = (bf16[1,128,6144]{2,1,0:T(8,128)(2,1)S(1)}, bf16[1,128,6144]{2,1,0:T(8,128)(2,1)}, u32[]{:S(2)}) copy-start(bf16[1,128,6144]{2,1,0:T(8,128)(2,1)} %param.9) | copy-start | bytes 4718596
  251.8 374.6 %copy-start.1 = (bf16[1,128,6144]{2,1,0:T(8,128)(2,1)S(1)}, bf16[1,128,6144]{2,1,0:T(8,128)(2,1)}, u32[]{:S(2)}) copy-start(bf16[1,128,6144]{2,1,0:T(8,128)(2,1)} %param.10) | copy-start | bytes 4718596
Sparse Core Ops, SparseCore 0:
  11.6 31.8 all-gather.5
  129.1 30.1 all-gather.7
  169.4 114.4 reduce-scatter.12
  286.6 111.6 reduce-scatter.6
  401.1 111.2 reduce-scatter.8
  515.1 111.2 reduce-scatter.10
